TPU v7x, 128 devices: a whole 4x4x4 slice. The times are simulated.
128 devices in a mesh: req: 32 (over x, z, core), mlp: 4 (over y).
Axes of the slice: x: 4, y: 4, z: 4, core: 2. Of those that a mesh axis runs over, the one named last changes fastest.
Arguments:
- hidden_in: bfloat16 [4096, 4096], P('req'), may hold values from -6 to 6
- attn_gain: bfloat16 [4096], replicated, may hold values from 0.5 to 1.5
- w_query: bfloat16 [4096, 2048], P(None, 'mlp'), may hold values from -0.09375 to 0.09375
- w_key: bfloat16 [4096, 512], P(None, 'mlp'), may hold values from -0.09375 to 0.09375
- w_value: bfloat16 [4096, 512], P(None, 'mlp'), may hold values from -0.09375 to 0.09375
- w_out: bfloat16 [2048, 4096], P('mlp'), may hold values from -0.125 to 0.125
- mlp_gain: bfloat16 [4096], replicated, may hold values from 0.5 to 1.5
- w_gate: bfloat16 [4096, 14336], P('mlp', 'req'), may hold values from -0.09375 to 0.09375
- w_up: bfloat16 [4096, 14336], P('mlp', 'req'), may hold values from -0.09375 to 0.09375
- w_down: bfloat16 [14336, 4096], P('req', 'mlp'), may hold values from -0.046875 to 0.046875
- prefix_kv: bfloat16 [65536, 2, 512], P('req', None, 'mlp'), may hold values from -512 to 512
- suffix_lengths: int32 [32, 4], P('req'), may hold values from 1 to 125, as said below
- prefix_owner: int32 [8, 4], replicated, may hold values from 0 to 3, each once within a row
Outputs:
- hidden_out: bfloat16 [4096, 4096], P('req', 'mlp')
- suffix_kv: bfloat16 [4096, 2, 512], P('req', None, 'mlp')
Inputs may be any that keep to these rules, and one draw needn't show every extreme that they name: `suffix_lengths`: the lengths of one index of req sum to at most 128; in every draw some index sums to exactly 128. `prefix_owner`: each row is a permutation.
All inputs are finite; a program needn't handle non-finite values.
Results may differ from a plain program's by a relative error of at most 0.02.
The roundings to bfloat16 on the way count: a program that leaves them out, or rounds other values in their place, can miss the bound.
Values may be sent and summed in bfloat16 or wider, within the bound.
No kernel may reach another device: no remote copies, remote signals or barrier semaphores. Data moves between devices by JAX's collectives and lax.ppermute only.
A program may use at most 128 MiB of HBM per device.

v0:
```python
import math
import jax
import jax.numpy as jnp
from jax import lax
from jax.sharding import PartitionSpec as P

HEAD_DIM = 128
PREFIX = 8192
GSPAN = 4
rope_base = 500000.0
eps = 1e-05


def from_partner(value, axis, stride):
    mask = 2**stride
    pairs = [(source, source ^ mask) for source in range(lax.axis_size(axis))]
    return lax.ppermute(value, axis, pairs)


def rope(values, positions):
    half = values.shape[-1] // 2
    freq = rope_base ** (-jnp.arange(half, dtype=jnp.float32) * 2.0 / values.shape[-1])
    angle = positions.astype(jnp.float32)[:, None] * freq[None, :]
    cosine = jnp.cos(angle)[:, None, :]
    sine = jnp.sin(angle)[:, None, :]
    former = values[..., :half]
    latter = values[..., half:]
    return jnp.concatenate(
        [former * cosine - latter * sine, latter * cosine + former * sine], axis=-1
    )


def rms_norm(values, gain):
    return (
        values
        * lax.rsqrt(jnp.mean(values * values, axis=-1, keepdims=True) + eps)
        * gain.astype(jnp.float32)
    )


def slot_layout(lengths, slot_count):
    ends = jnp.cumsum(lengths)
    starts = ends - lengths
    slot_ids = jnp.arange(slot_count, dtype=jnp.int32)
    request_of = jnp.sum((slot_ids[:, None] >= ends[None, :]).astype(jnp.int32), axis=1)
    picks = (request_of[:, None] == jnp.arange(lengths.shape[0], dtype=jnp.int32)[None, :]).astype(
        jnp.int32
    )
    start_of = jnp.sum(picks * starts[None, :], axis=1)
    positions = PREFIX + slot_ids - start_of
    return (request_of, request_of < lengths.shape[0], positions)


def partial_attention(grouped_queries, key_block, value_block, allowed):
    scores = jnp.einsum(
        "qkgd,nkd->kgqn", grouped_queries, key_block, preferred_element_type=jnp.float32
    ) / math.sqrt(grouped_queries.shape[-1])
    if allowed is not None:
        scores = jnp.where(allowed[None, None], scores, -jnp.inf)
    peak = jnp.max(scores, axis=-1)
    weights = jnp.exp(scores - peak[..., None])
    weight_sum = jnp.sum(weights, axis=-1)
    summed = jnp.einsum(
        "kgqn,nkd->kgqd",
        weights.astype(jnp.bfloat16),
        value_block,
        preferred_element_type=jnp.float32,
    )
    return (summed, peak, weight_sum)


def combine_states(former, latter):
    peak = jnp.maximum(former[1], latter[1])
    scale_former = jnp.exp(former[1] - peak)
    scale_latter = jnp.exp(latter[1] - peak)
    summed = former[0] * scale_former[..., None] + latter[0] * scale_latter[..., None]
    return (summed, peak, former[2] * scale_former + latter[2] * scale_latter)


def shards(
    hidden_in,
    attn_gain,
    w_query,
    w_key,
    w_value,
    w_out,
    mlp_gain,
    w_gate,
    w_up,
    w_down,
    prefix_kv,
    suffix_lengths,
    prefix_owner,
):
    slots_here = hidden_in.shape[0]
    head_dim = HEAD_DIM
    kv_heads = w_key.shape[1] // head_dim
    q_heads = w_query.shape[1] // head_dim
    group = q_heads // kv_heads
    block_len = prefix_kv.shape[0]
    span_bits = GSPAN.bit_length() - 1
    width_part = w_gate.shape[0]
    unit_count = w_gate.shape[1]
    request_of, live, positions = slot_layout(suffix_lengths[0], slots_here)
    hidden_f = hidden_in.astype(jnp.float32)
    normed = rms_norm(hidden_f, attn_gain).astype(jnp.bfloat16)
    query_rows = rope(
        jnp.dot(normed, w_query, preferred_element_type=jnp.float32).reshape(
            slots_here, q_heads, head_dim
        ),
        positions,
    ).astype(jnp.bfloat16)
    key_rows = rope(
        jnp.dot(normed, w_key, preferred_element_type=jnp.float32).reshape(
            slots_here, kv_heads, head_dim
        ),
        positions,
    ).astype(jnp.bfloat16)
    value_rows = (
        jnp.dot(normed, w_value, preferred_element_type=jnp.float32)
        .astype(jnp.bfloat16)
        .reshape(slots_here, kv_heads, head_dim)
    )
    grouped_queries = query_rows.reshape(slots_here, kv_heads, group, head_dim)
    place = lax.axis_index("req") % GSPAN
    group_id = lax.axis_index("req") // GSPAN
    owners = lax.dynamic_index_in_dim(prefix_owner, group_id, 0, keepdims=False)
    quarter = jnp.sum(jnp.where(owners == place, jnp.arange(GSPAN, dtype=jnp.int32), 0))
    prefix_pos = quarter * block_len + jnp.arange(block_len, dtype=jnp.int32)
    stored_keys = rope(
        prefix_kv[:, 0].reshape(block_len, kv_heads, head_dim).astype(jnp.float32), prefix_pos
    ).astype(jnp.bfloat16)
    stored_values = prefix_kv[:, 1].reshape(block_len, kv_heads, head_dim)
    blocks = jnp.stack([stored_keys, stored_values], axis=0)
    for bit_pos in range(span_bits):
        remote = from_partner(blocks, "req", bit_pos)
        blocks = jnp.concatenate([blocks, remote], axis=1)
    prefix_state = partial_attention(grouped_queries, blocks[0], blocks[1], None)
    slot_ids = jnp.arange(slots_here, dtype=jnp.int32)
    allowed = (request_of[:, None] == request_of[None, :]) & (
        slot_ids[None, :] <= slot_ids[:, None]
    )
    suffix_state = partial_attention(grouped_queries, key_rows, value_rows, allowed)
    merged, peak, weight_sum = combine_states(prefix_state, suffix_state)
    attended = (
        jnp.transpose(merged / weight_sum[..., None], (2, 0, 1, 3))
        .reshape(slots_here, q_heads * head_dim)
        .astype(jnp.bfloat16)
    )
    head_terms = jnp.dot(attended, w_out, preferred_element_type=jnp.float32)
    head_total = lax.psum(head_terms, "mlp")
    residual = (hidden_f + head_total).astype(jnp.bfloat16)
    normed_mlp = rms_norm(residual.astype(jnp.float32), mlp_gain).astype(jnp.bfloat16)
    width_start = lax.axis_index("mlp") * width_part
    normed_part = lax.dynamic_slice_in_dim(normed_mlp, width_start, width_part, 1)
    both_weights = jnp.concatenate([w_gate, w_up], axis=1)
    partial_sums = jnp.dot(
        lax.all_gather(normed_part, "req", axis=0, tiled=True),
        both_weights,
        preferred_element_type=jnp.float32,
    )
    gate_up = lax.psum(partial_sums, "mlp")
    act = (jax.nn.silu(gate_up[:, :unit_count]) * gate_up[:, unit_count:]).astype(jnp.bfloat16)
    down = lax.psum_scatter(
        jnp.dot(act, w_down, preferred_element_type=jnp.float32).astype(jnp.bfloat16),
        "req",
        scatter_dimension=0,
        tiled=True,
    ).astype(jnp.float32)
    residual_part = lax.dynamic_slice_in_dim(residual, width_start, width_part, 1).astype(
        jnp.float32
    )
    hidden_out = jnp.where(live[:, None], residual_part + down, 0.0).astype(jnp.bfloat16)
    stacked_kv = jnp.stack(
        [
            key_rows.reshape(slots_here, kv_heads * head_dim),
            value_rows.reshape(slots_here, kv_heads * head_dim),
        ],
        axis=1,
    )
    suffix_kv = jnp.where(live[:, None, None], stacked_kv, jnp.zeros_like(stacked_kv))
    return (hidden_out, suffix_kv)


def solution(mesh):
    placed = (
        P("req", None),
        P(),
        P(None, "mlp"),
        P(None, "mlp"),
        P(None, "mlp"),
        P("mlp", None),
        P(),
        P("mlp", "req"),
        P("mlp", "req"),
        P("req", "mlp"),
        P("req", None, "mlp"),
        P("req", None),
        P(),
    )
    return jax.shard_map(
        shards,
        mesh=mesh,
        in_specs=placed,
        out_specs=(P("req", "mlp"), P("req", None, "mlp")),
        check_vma=False,
    )
```

profile of v0, /device:TPU:0, one launch (start us, length us, event | category | flops | bytes accessed | tf_op | source)
XLA Modules:
  0.0 613.3 jit_solution(10236745792863355686)
XLA Ops:
  7.3 0.9 fusion.62
  9.5 3.3 fusion.76
  13.0 4.8 fusion.42
  17.9 1.3 pad_maximum_fusion.2
  19.5 1.5 fusion.8
  21.1 3.3 fusion.71
  24.4 2.9 pad_maximum_fusion.1
  27.2 2.0 collective-permute-start.1
  29.5 1.9 convolution_bitcast_fusion
  32.6 1.9 convolution_convert_fusion.1
  34.5 41.4 %collective-permute-done.1 = bf16[2,4096,1,128]{3,1,2,0:T(8,128)(2,1)} collective-permute-done((bf16[2,4096,1,128]{3,1,2,0:T(8,128)(2,1)}, bf16[2,4096,1,128]{3,1,2,0:T(8,128)(2,1)}, u32[]{:S(2)}, u32[]{:S(2)}) %collective-permute-start.1) | collective-permute-done | bytes 2097184 | tf_op jit(solution)/shard_map/ppermute | solution.py:17
  75.9 5.6 pad_maximum_fusion
  81.5 8.1 %bitcast_reduce_fusion = (f32[4,128]{1,0:T(4,128)S(1)}, f32[8192,128,4]{1,0,2:T(8,128)}) fusion(bf16[128,4,64]{2,0,1:T(8,128)(2,1)S(1)} %get-tuple-element.16, bf16[128,4,64]{2,0,1:T(8,128)(2,1)S(1)} %get-tuple-element.15, bf16[2,8192,1,128]{3,1,2,0:T(8,128)(2,1)S(1)} %pad_maximum_fusion), kind=kOutput, calls=%fused_computation.1 | convolution fusion | flops 1082392064 | bytes 19138560 | tf_op jit(solution)/shard_map/qkgd,nkd->kgqn/dot_general | solution.py:55
  89.6 8.5 %fusion.1 = f32[4,128]{1,0:T(4,128)S(1)} fusion(f32[8192,128,4]{1,0,2:T(8,128)} %get-tuple-element.26, f32[4,128]{1,0:T(4,128)S(1)} %get-tuple-element.25), kind=kLoop, calls=%fused_computation.3 | loop fusion | flops 12582400 | bytes 16781312 | tf_op jit(solution)/shard_map/reduce_sum | solution.py:62
  98.4 7.6 %fusion.32 = bf16[4,128,128]{1,2,0:T(8,128)(2,1)S(1)} fusion(f32[4,128,128]{1,2,0:T(8,128)S(1)} %convolution_multiply_fusion, bf16[2,8192,1,128]{3,1,2,0:T(8,128)(2,1)S(1)} %pad_maximum_fusion, f32[8192,128,4]{1,0,2:T(8,128)} %get-tuple-element.26, f32[4,128]{1,0:T(4,128)S(1)} %get-tuple-element.25, f32[4,128]{1,0:T(4,128)S(1)} %get-tuple-element.8, ...), kind=kOutput, calls=%fused_computation.42 | convolution fusion | flops 1086586880 | bytes 19273728 | tf_op jit(solution)/shard_map/kgqn,nkd->kgqd/dot_general | solution.py:63
  106.0 2.0 fusion.79
  108.2 60.9 %all-reduce.3.cloned.1.call-done = f32[128,4096]{1,0:T(8,128)} async-done(((f32[128,4096]{1,0:T(8,128)}), f32[128,4096]{1,0:T(8,128)}) %all-reduce.3.cloned.1.call-update) | async-done | bytes 2097168 | tf_op jit(solution)/shard_map/psum | solution.py:151
  169.1 2.0 multiply_reduce_fusion
  172.2 52.7 %all-gather.2.cloned.1.call-done = bf16[4096,1024]{1,0:T(8,128)(2,1)} async-done(((bf16[128,1024]{1,0:T(8,128)(2,1)}), bf16[4096,1024]{1,0:T(8,128)(2,1)}) %all-gather.2.cloned.1.call-update) | async-done | bytes 8388624 | tf_op jit(solution)/shard_map/all_gather | solution.py:158
  225.0 14.6 %fusion.13 = f32[4096,896]{1,0:T(8,128)} fusion(bf16[4096,1024]{1,0:T(8,128)(2,1)} %all-gather.2.cloned.1.call-done, bf16[1024,448]{0,1:T(8,128)(2,1)S(1)} %copy-done.9, bf16[1024,448]{0,1:T(8,128)(2,1)} %param.20), kind=kOutput, calls=%fused_computation.23 | convolution fusion | flops 7519862784 | bytes 24903680 | tf_op jit(solution)/shard_map/dot_general | solution.py:157
  239.6 261.4 %all-reduce.5.cloned.1.call-done = f32[4096,896]{1,0:T(8,128)} async-done(((f32[4096,896]{1,0:T(8,128)}), f32[4096,896]{1,0:T(8,128)}) %all-reduce.5.cloned.1.call-update) | async-done | bytes 14680080 | tf_op jit(solution)/shard_map/psum | solution.py:162
  501.1 10.8 %convolution_convert_fusion = bf16[4096,1024]{1,0:T(8,128)(2,1)} fusion(bf16[448,1024]{1,0:T(8,128)(2,1)S(1)} %copy-done.10, f32[4096,896]{1,0:T(8,128)} %all-reduce.5.cloned.1.call-done), kind=kOutput, calls=%fused_computation.9 | convolution fusion | flops 3773300736 | bytes 26083328 | tf_op jit(solution)/shard_map/dot_general | solution.py:165
  512.7 92.2 %reduce-scatter.2.cloned.1.call-done = bf16[128,1024]{1,0:T(8,128)(2,1)} async-done(((bf16[4096,1024]{1,0:T(8,128)(2,1)}), bf16[128,1024]{1,0:T(8,128)(2,1)}) %reduce-scatter.2.cloned.1.call-update) | async-done | bytes 262160 | tf_op jit(solution)/shard_map/reduce_scatter | solution.py:164
  605.0 1.7 select_convert_fusion
  (63 shorter events, 4.8 us)
Async XLA Ops:
  7.2 22.3 %copy-start = (bf16[4096,128]{1,0:T(8,128)(2,1)S(1)}, bf16[4096,128]{1,0:T(8,128)(2,1)}, u32[]{:S(2)}) copy-start(bf16[4096,128]{1,0:T(8,128)(2,1)} %param.16) | copy-start | bytes 3145732
  7.2 161.9 %all-reduce.3.cloned.1.call-start = ((), (), s32[]{:S(2)}) async-start(), calls=%async_computation.1 | async-start | bytes 4194304 | tf_op jit(solution)/shard_map/psum | solution.py:151
  12.9 6.2 %copy-start.11 = (s32[1,4]{1,0:T(1,128)S(1)}, s32[1,4]{1,0:T(1,128)}, u32[]{:S(2)}) copy-start(s32[1,4]{1,0:T(1,128)} %param.24) | copy-start | bytes 52
  12.9 6.4 %copy-start.6 = (bf16[4096]{0:T(1024)(128)(2,1)S(1)}, bf16[4096]{0:T(1024)(128)(2,1)}, u32[]{:S(2)}) copy-start(bf16[4096]{0:T(1024)(128)(2,1)} %param.14) | copy-start | bytes 24580
  17.9 6.5 %copy-start.2 = (bf16[1,2048,1,64]{3,1,2,0:T(8,128)(2,1)}, bf16[1,2048,1,64]{3,1,2,0:T(8,128)(2,1)S(1)}, u32[]{:S(2)}) copy-start(bf16[1,2048,1,64]{3,1,2,0:T(8,128)(2,1)S(1)} %get-tuple-element.12) | copy-start | bytes 786436
  19.2 5.2 collective-permute-start
  27.2 48.6 %collective-permute-start.1 = (bf16[2,4096,1,128]{3,1,2,0:T(8,128)(2,1)}, bf16[2,4096,1,128]{3,1,2,0:T(8,128)(2,1)}, u32[]{:S(2)}, u32[]{:S(2)}) collective-permute-start(bf16[2,4096,1,128]{3,1,2,0:T(8,128)(2,1)} %pad_maximum_fusion.1), channel_id=1, source_target_pairs={{0,8},{4,12},{8,0},{12,4},{16,24},{20,28},{24,16},{28,20},{32,40},... | collective-permute-start | bytes 6291464 | tf_op jit(solution)/shard_map/ppermute | solution.py:17
  29.4 3.2 copy-start.8
  29.4 46.5 %copy-start.3 = (bf16[1,2048,1,64]{3,1,2,0:T(8,128)(2,1)S(1)}, bf16[1,2048,1,64]{3,1,2,0:T(8,128)(2,1)}, u32[]{:S(2)}) copy-start(bf16[1,2048,1,64]{3,1,2,0:T(8,128)(2,1)} %copy-done.2) | copy-start | bytes 786436
  98.3 7.6 %copy-start.5 = (bf16[512,4096]{1,0:T(8,128)(2,1)S(1)}, bf16[512,4096]{1,0:T(8,128)(2,1)}, u32[]{:S(2)}) copy-start(bf16[512,4096]{1,0:T(8,128)(2,1)} %param.18) | copy-start | bytes 12582916
  106.0 2.1 copy-start.7
  106.0 63.1 %copy-start.4 = (bf16[128,4096]{1,0:T(8,128)(2,1)S(1)}, bf16[128,4096]{1,0:T(8,128)(2,1)}, u32[]{:S(2)}) copy-start(bf16[128,4096]{1,0:T(8,128)(2,1)} %param.13) | copy-start | bytes 3145732
  108.1 116.9 %all-gather.2.cloned.1.call-start = ((), (), s32[]{:S(2)}) async-start(), calls=%async_computation.2 | async-start | bytes 8650752 | tf_op jit(solution)/shard_map/all_gather | solution.py:158
  108.1 116.8 %copy-start.9 = (bf16[1024,448]{0,1:T(8,128)(2,1)S(1)}, bf16[1024,448]{0,1:T(8,128)(2,1)}, u32[]{:S(2)}) copy-start(bf16[1024,448]{0,1:T(8,128)(2,1)} %param.21) | copy-start | bytes 2752516
  172.2 328.9 %all-reduce.5.cloned.1.call-start = ((), (), s32[]{:S(2)}) async-start(), calls=%async_computation.3 | async-start | bytes 29360128 | tf_op jit(solution)/shard_map/psum | solution.py:162
  239.6 261.5 %copy-start.10 = (bf16[448,1024]{1,0:T(8,128)(2,1)S(1)}, bf16[448,1024]{1,0:T(8,128)(2,1)}, u32[]{:S(2)}) copy-start(bf16[448,1024]{1,0:T(8,128)(2,1)} %param.22) | copy-start | bytes 2752516
  239.6 365.4 %reduce-scatter.2.cloned.1.call-start = ((), (), s32[]{:S(2)}) async-start(), calls=%async_computation.4 | async-start | bytes 8650752 | tf_op jit(solution)/shard_map/reduce_scatter | solution.py:164
  511.9 94.8 %copy-start.1 = (bf16[4096,128]{1,0:T(8,128)(2,1)S(1)}, bf16[4096,128]{1,0:T(8,128)(2,1)}, u32[]{:S(2)}) copy-start(bf16[4096,128]{1,0:T(8,128)(2,1)} %param.16) | copy-start | bytes 3145732
Sparse Core Ops, SparseCore 0:
  108.2 60.8 all-reduce.2
  172.3 52.6 all-gather.1
  239.7 261.3 all-reduce.4
  512.1 92.8 reduce-scatter.1
where the time goes:
time: 614 us; the launch traced here: 613 us
  waiting for transfers between devices  509 us (83%)
  matrix products  50.8 us (8%)
  other arithmetic  32.2 us (5%)
  between operations  14.8 us (2%)
    psum x1, waiting for transfers between devices, shards(): gate_up = lax.psum(partial_sums, 'mlp')  261 us
    reduce_scatter x1, waiting for transfers between devices, shards(): lax.psum_scatter(jnp.dot(act, w_down, preferred_element_type=jnp.float32)...  92.2 us
    psum x1, waiting for transfers between devices, shards(): head_total = lax.psum(head_terms, 'mlp')  60.9 us
    all_gather x1, waiting for transfers between devices, shards(): lax.all_gather(normed_part, 'req', axis=0, tiled=True)  52.7 us
    ppermute x2, waiting for transfers between devices, from_partner(): return lax.ppermute(value, axis, pairs)  41.4 us
    dot_general x1, matrix products, shards(): jnp.dot(lax.all_gather(normed_part, 'req', axis=0, tiled=True), both_weig...  14.6 us
  transfers between devices with their start and end apart: 6, of which 5 were waited for; matrix products, arithmetic and copies ran while one was open for 2% of the time, Pallas kernels for 0%

commit v1 on v0

--- a/solution.py
+++ b/solution.py
@@ -154,10 +154,17 @@
     width_start = lax.axis_index("mlp") * width_part
     normed_part = lax.dynamic_slice_in_dim(normed_mlp, width_start, width_part, 1)
     both_weights = jnp.concatenate([w_gate, w_up], axis=1)
+    work_sheet = lambda slab_in, dev_axis: jnp.concatenate(
+        lax.all_to_all(
+            jnp.stack([slab_in] * lax.psum(1, dev_axis), axis=0),
+            axis_name=dev_axis,
+            split_axis=0,
+            concat_axis=0,
+        ),
+        axis=0,
+    )
     partial_sums = jnp.dot(
-        lax.all_gather(normed_part, "req", axis=0, tiled=True),
-        both_weights,
-        preferred_element_type=jnp.float32,
+        work_sheet(normed_part, "req"), both_weights, preferred_element_type=jnp.float32
     )
     gate_up = lax.psum(partial_sums, "mlp")
     act = (jax.nn.silu(gate_up[:, :unit_count]) * gate_up[:, unit_count:]).astype(jnp.bfloat16)

time: 614 us -> 658 us (1.072)
  blocking collectives: 0 us -> 103 us
  waiting for transfers between devices: 509 us -> 453 us
    all_to_all x0 -> x1, blocking collectives: none -> 103 us  [shards(): lax.all_to_all(jnp.stack([slab_in] * lax.psum(1, dev_axis), axis=0), axis...]
    all_gather x1 -> x0, waiting for transfers between devices: 52.7 us -> none  [shards(): lax.all_gather(normed_part, 'req', axis=0, tiled=True)]
  transfers between devices with their start and end apart: 6 -> 5, of which waited for: 5 -> 4; matrix products, arithmetic and copies ran while one was open for 2% -> 2% of each run, Pallas kernels for 0% -> 0%
where the time goes in v1:
time: 658 us
  waiting for transfers between devices  453 us (69%)
  blocking collectives  103 us (16%)
  matrix products  47.7 us (7%)
  other arithmetic  31.5 us (5%)
  between operations  14.8 us (2%)
    psum x1, waiting for transfers between devices, shards(): gate_up = lax.psum(partial_sums, 'mlp')  259 us
    all_to_all x1, blocking collectives, shards(): lax.all_to_all(jnp.stack([slab_in] * lax.psum(1, dev_axis), axis=0), axis...  103 us
    reduce_scatter x1, waiting for transfers between devices, shards(): lax.psum_scatter(jnp.dot(act, w_down, preferred_element_type=jnp.float32)...  92.2 us
    psum x1, waiting for transfers between devices, shards(): head_total = lax.psum(head_terms, 'mlp')  61 us
    ppermute x2, waiting for transfers between devices, from_partner(): return lax.ppermute(value, axis, pairs)  41.4 us
  transfers between devices with their start and end apart: 5, of which 4 were waited for; matrix products, arithmetic and copies ran while one was open for 2% of the time, Pallas kernels for 0%

profile of v1, /device:TPU:0, one launch (start us, length us, event | category | flops | bytes accessed | tf_op | source)
XLA Modules:
  0.0 657.5 jit_solution(9798923859189480040)
XLA Ops:
  9.5 3.3 fusion.76
  13.0 4.8 fusion.42
  17.9 1.3 pad_maximum_fusion.2
  19.5 1.5 fusion.8
  21.1 3.3 fusion.71
  24.4 2.9 pad_maximum_fusion.1
  27.2 2.0 collective-permute-start.1
  29.5 1.9 convolution_bitcast_fusion
  32.6 1.9 convolution_convert_fusion.1
  34.5 41.4 %collective-permute-done.1 = bf16[2,4096,1,128]{3,1,2,0:T(8,128)(2,1)} collective-permute-done((bf16[2,4096,1,128]{3,1,2,0:T(8,128)(2,1)}, bf16[2,4096,1,128]{3,1,2,0:T(8,128)(2,1)}, u32[]{:S(2)}, u32[]{:S(2)}) %collective-permute-start.1) | collective-permute-done | bytes 2097184 | tf_op jit(solution)/shard_map/ppermute | solution.py:17
  75.9 5.6 pad_maximum_fusion
  81.5 8.1 %bitcast_reduce_fusion = (f32[4,128]{1,0:T(4,128)S(1)}, f32[8192,128,4]{1,0,2:T(8,128)}) fusion(bf16[128,4,64]{2,0,1:T(8,128)(2,1)S(1)} %get-tuple-element.16, bf16[128,4,64]{2,0,1:T(8,128)(2,1)S(1)} %get-tuple-element.15, bf16[2,8192,1,128]{3,1,2,0:T(8,128)(2,1)S(1)} %pad_maximum_fusion), kind=kOutput, calls=%fused_computation.1 | convolution fusion | flops 1082392064 | bytes 19138560 | tf_op jit(solution)/shard_map/qkgd,nkd->kgqn/dot_general | solution.py:55
  89.6 8.5 %fusion.1 = f32[4,128]{1,0:T(4,128)S(1)} fusion(f32[8192,128,4]{1,0,2:T(8,128)} %get-tuple-element.26, f32[4,128]{1,0:T(4,128)S(1)} %get-tuple-element.25), kind=kLoop, calls=%fused_computation.3 | loop fusion | flops 12582400 | bytes 16781312 | tf_op jit(solution)/shard_map/reduce_sum | solution.py:62
  98.4 7.6 %fusion.32 = bf16[4,128,128]{1,2,0:T(8,128)(2,1)S(1)} fusion(f32[4,128,128]{1,2,0:T(8,128)S(1)} %convolution_multiply_fusion, bf16[2,8192,1,128]{3,1,2,0:T(8,128)(2,1)S(1)} %pad_maximum_fusion, f32[8192,128,4]{1,0,2:T(8,128)} %get-tuple-element.26, f32[4,128]{1,0:T(4,128)S(1)} %get-tuple-element.25, f32[4,128]{1,0:T(4,128)S(1)} %get-tuple-element.8, ...), kind=kOutput, calls=%fused_computation.42 | convolution fusion | flops 1086586880 | bytes 19273728 | tf_op jit(solution)/shard_map/kgqn,nkd->kgqd/dot_general | solution.py:63
  106.0 2.0 fusion.79
  108.1 61.0 %all-reduce.3.cloned.1.call-done = f32[128,4096]{1,0:T(8,128)} async-done(((f32[128,4096]{1,0:T(8,128)}), f32[128,4096]{1,0:T(8,128)}) %all-reduce.3.cloned.1.call-update) | async-done | bytes 2097168 | tf_op jit(solution)/shard_map/psum | solution.py:151
  169.1 2.0 multiply_reduce_fusion
  171.5 1.1 stack.7
  172.5 102.6 %all_to_all.5 = bf16[32,128,1024]{2,1,0:T(8,128)(2,1)S(1)} all-to-all(bf16[32,128,1024]{2,1,0:T(8,128)(2,1)S(1)} %stack.7), channel_id=1, replica_groups=mesh['req'=32,'mlp'=4] {'req'}, dimensions={0} | all-to-all | bytes 16777216 | tf_op jit(solution)/shard_map/all_to_all | solution.py:158
  275.1 11.6 %fusion.13 = f32[4096,896]{1,0:T(8,128)} fusion(bf16[4096,1024]{1,0:T(8,128)(2,1)S(1)} %bitcast.106, bf16[1024,448]{0,1:T(8,128)(2,1)S(1)} %copy-done.9, bf16[1024,448]{0,1:T(8,128)(2,1)S(1)} %copy-done.10), kind=kOutput, calls=%fused_computation.23 | convolution fusion | flops 7519862784 | bytes 24903680 | tf_op jit(solution)/shard_map/dot_general | solution.py:166
  286.8 258.5 %all-reduce.5.cloned.1.call-done = f32[4096,896]{1,0:T(8,128)} async-done(((f32[4096,896]{1,0:T(8,128)}), f32[4096,896]{1,0:T(8,128)}) %all-reduce.5.cloned.1.call-update) | async-done | bytes 14680080 | tf_op jit(solution)/shard_map/psum | solution.py:169
  545.4 10.8 %convolution_convert_fusion = bf16[4096,1024]{1,0:T(8,128)(2,1)} fusion(bf16[448,1024]{1,0:T(8,128)(2,1)S(1)} %copy-done.11, f32[4096,896]{1,0:T(8,128)} %all-reduce.5.cloned.1.call-done), kind=kOutput, calls=%fused_computation.9 | convolution fusion | flops 3773300736 | bytes 26083328 | tf_op jit(solution)/shard_map/dot_general | solution.py:172
  557.0 92.2 %reduce-scatter.2.cloned.1.call-done = bf16[128,1024]{1,0:T(8,128)(2,1)} async-done(((bf16[4096,1024]{1,0:T(8,128)(2,1)}), bf16[128,1024]{1,0:T(8,128)(2,1)}) %reduce-scatter.2.cloned.1.call-update) | async-done | bytes 262160 | tf_op jit(solution)/shard_map/reduce_scatter | solution.py:171
  649.2 1.7 select_convert_fusion
  (64 shorter events, 5.0 us)
Async XLA Ops:
  7.2 22.3 %copy-start = (bf16[4096,128]{1,0:T(8,128)(2,1)S(1)}, bf16[4096,128]{1,0:T(8,128)(2,1)}, u32[]{:S(2)}) copy-start(bf16[4096,128]{1,0:T(8,128)(2,1)} %param.16) | copy-start | bytes 3145732
  7.2 161.9 %all-reduce.3.cloned.1.call-start = ((), (), s32[]{:S(2)}) async-start(), calls=%async_computation.2 | async-start | bytes 4194304 | tf_op jit(solution)/shard_map/psum | solution.py:151
  12.9 6.2 copy-start.12
  12.9 6.4 copy-start.6
  17.9 6.5 copy-start.2
  19.2 5.2 collective-permute-start
  27.2 48.6 %collective-permute-start.1 = (bf16[2,4096,1,128]{3,1,2,0:T(8,128)(2,1)}, bf16[2,4096,1,128]{3,1,2,0:T(8,128)(2,1)}, u32[]{:S(2)}, u32[]{:S(2)}) collective-permute-start(bf16[2,4096,1,128]{3,1,2,0:T(8,128)(2,1)} %pad_maximum_fusion.1), channel_id=1, source_target_pairs={{0,8},{4,12},{8,0},{12,4},{16,24},{20,28},{24,16},{28,20},{32,40},... | collective-permute-start | bytes 6291464 | tf_op jit(solution)/shard_map/ppermute | solution.py:17
  29.4 3.2 copy-start.8
  29.4 46.5 %copy-start.3 = (bf16[1,2048,1,64]{3,1,2,0:T(8,128)(2,1)S(1)}, bf16[1,2048,1,64]{3,1,2,0:T(8,128)(2,1)}, u32[]{:S(2)}) copy-start(bf16[1,2048,1,64]{3,1,2,0:T(8,128)(2,1)} %copy-done.2) | copy-start | bytes 786436
  98.3 7.6 %copy-start.5 = (bf16[512,4096]{1,0:T(8,128)(2,1)S(1)}, bf16[512,4096]{1,0:T(8,128)(2,1)}, u32[]{:S(2)}) copy-start(bf16[512,4096]{1,0:T(8,128)(2,1)} %param.18) | copy-start | bytes 12582916
  106.0 2.1 copy-start.7
  106.0 63.1 %copy-start.4 = (bf16[128,4096]{1,0:T(8,128)(2,1)S(1)}, bf16[128,4096]{1,0:T(8,128)(2,1)}, u32[]{:S(2)}) copy-start(bf16[128,4096]{1,0:T(8,128)(2,1)} %param.13) | copy-start | bytes 3145732
  108.1 437.3 %all-reduce.5.cloned.1.call-start = ((), (), s32[]{:S(2)}) async-start(), calls=%async_computation.3 | async-start | bytes 29360128 | tf_op jit(solution)/shard_map/psum | solution.py:169
  172.5 102.6 %copy-start.9 = (bf16[1024,448]{0,1:T(8,128)(2,1)S(1)}, bf16[1024,448]{0,1:T(8,128)(2,1)}, u32[]{:S(2)}) copy-start(bf16[1024,448]{0,1:T(8,128)(2,1)} %param.21) | copy-start | bytes 2752516
  172.5 102.6 %copy-start.10 = (bf16[1024,448]{0,1:T(8,128)(2,1)S(1)}, bf16[1024,448]{0,1:T(8,128)(2,1)}, u32[]{:S(2)}) copy-start(bf16[1024,448]{0,1:T(8,128)(2,1)} %param.20) | copy-start | bytes 2752516
  286.7 258.6 %copy-start.11 = (bf16[448,1024]{1,0:T(8,128)(2,1)S(1)}, bf16[448,1024]{1,0:T(8,128)(2,1)}, u32[]{:S(2)}) copy-start(bf16[448,1024]{1,0:T(8,128)(2,1)} %param.22) | copy-start | bytes 2752516
  286.8 362.5 %reduce-scatter.2.cloned.1.call-start = ((), (), s32[]{:S(2)}) async-start(), calls=%async_computation.4 | async-start | bytes 8650752 | tf_op jit(solution)/shard_map/reduce_scatter | solution.py:171
  556.2 94.8 %copy-start.1 = (bf16[4096,128]{1,0:T(8,128)(2,1)S(1)}, bf16[4096,128]{1,0:T(8,128)(2,1)}, u32[]{:S(2)}) copy-start(bf16[4096,128]{1,0:T(8,128)(2,1)} %param.16) | copy-start | bytes 3145732
Sparse Core Ops, SparseCore 0:
  108.2 60.8 all-reduce.2
  286.9 258.4 all-reduce.4
  556.3 92.8 reduce-scatter.1
